TPU v7x, 256 devices: a whole 4x4x8 slice. The times are simulated.
256 devices in a mesh: date: 64 (over x, y, z_lo, core), rng: 4 (over z_hi).
Axes of the slice: x: 4, y: 4, z: 8 (z_hi: 4, z_lo: 2; z = z_hi * 2 + z_lo), core: 2. Of those that a mesh axis runs over, the one named last changes fastest.
Arguments:
- slc_re: bfloat16 [64, 2048, 512], P('date', None, 'rng'), may hold values from -170 to 170
- slc_im: bfloat16 [64, 2048, 512], P('date', None, 'rng'), may hold values from -170 to 170
- ref_date: int32 [1], replicated, may hold values from 0 to 63
- gain: float32 [2048], replicated, may hold values from 0.25 to 2
- bperp: int32 [64], replicated, may hold values from -200 to 199
- tdays: int32 [64], replicated, may hold values from 0 to 1899
- mask: int32 [2048, 512], P(None, 'rng'), may hold values from 0 to 1, as said below
Outputs:
- periodogram: float32 [2048, 512, 256], P('date', 'rng')
Inputs may be any that keep to these rules, and one draw needn't show every extreme that they name: `mask`: each aligned block of 32 lines by 128 range columns holds exactly 1024 candidates.
All inputs are finite; a program needn't handle non-finite values.
Results may differ from a plain program's by a relative error of at most 0.0067.
Values may be sent and summed in bfloat16 or wider, within the bound.
No kernel may reach another device: no remote copies, remote signals or barrier semaphores. Data moves between devices by JAX's collectives and lax.ppermute only.
A program may use at most 64 MiB of HBM per device.

v0:
```python
import math
import jax
import jax.numpy as jnp
from jax import lax
from jax.sharding import PartitionSpec as P

HGRID = 16
VGRID = 16
PHASE_Q = 1024


def broadcast(shard, axis, root):
    mine = lax.axis_index(axis) == root
    return lax.psum(jnp.where(mine, shard, jnp.zeros_like(shard)), axis)


def dft_tables(length):
    positions = jnp.arange(length, dtype=jnp.int32)
    products = positions[:, None] * positions[None, :] % length
    angles = products.astype(jnp.float32) * (2.0 * math.pi / length)
    return (jnp.cos(angles).astype(jnp.bfloat16), jnp.sin(angles).astype(jnp.bfloat16))


def phase_tables(bperp, tdays):
    grid_points = jnp.arange(HGRID * VGRID, dtype=jnp.int32)
    height_step = grid_points // VGRID
    speed_step = grid_points % VGRID
    quanta = (
        bperp[:, None] * height_step[None, :] + tdays[:, None] * speed_step[None, :]
    ) % PHASE_Q
    angles = quanta.astype(jnp.float32) * (2.0 * math.pi / PHASE_Q)
    phase_re = jnp.cos(angles).astype(jnp.bfloat16)
    phase_im = jnp.sin(angles).astype(jnp.bfloat16)
    upper = jnp.concatenate([phase_re, -phase_im], axis=1)
    lower = jnp.concatenate([phase_im, phase_re], axis=1)
    return jnp.concatenate([upper, lower], axis=0)


def coherence_map(piece_re, piece_im, phase_table):
    date_count = piece_re.shape[0]
    grid_size = phase_table.shape[1] // 2
    stacked = jnp.concatenate([piece_re, piece_im], axis=0)
    spectra = lax.dot_general(
        stacked, phase_table, (((0,), (0,)), ((), ())), preferred_element_type=jnp.float32
    )
    peri_re = spectra[:, :grid_size]
    peri_im = spectra[:, grid_size:]
    wide_re = piece_re.astype(jnp.float32)
    wide_im = piece_im.astype(jnp.float32)
    pixel_power = jnp.sum(wide_re * wide_re + wide_im * wide_im, axis=0) / date_count
    return (peri_re * peri_re + peri_im * peri_im) / (date_count * jnp.maximum(pixel_power, 1.0))[
        :, None
    ]


def shards(slc_re, slc_im, ref_date, gain, bperp, tdays, mask):
    date_dev, lines, rg_dev = slc_re.shape
    date_axis = lax.axis_size("date")
    pixel_total = lines * rg_dev * lax.axis_size("rng")
    ref_index = ref_date[0]
    owner_index = ref_index // date_dev
    owner_slot = ref_index % date_dev
    own_re = lax.dynamic_index_in_dim(slc_re, owner_slot, 0, keepdims=False)
    own_im = lax.dynamic_index_in_dim(slc_im, owner_slot, 0, keepdims=False)
    ref_re, ref_im = (
        broadcast(own_re, "date", owner_index),
        broadcast(own_im, "date", owner_index),
    )
    wide_re = slc_re.astype(jnp.float32)
    wide_im = slc_im.astype(jnp.float32)
    ref_wide_re = ref_re.astype(jnp.float32)
    ref_wide_im = ref_im.astype(jnp.float32)
    local_sums = jnp.sum(wide_re * wide_re + wide_im * wide_im, axis=(1, 2))
    ref_local = jnp.sum(ref_wide_re * ref_wide_re + ref_wide_im * ref_wide_im)
    date_sums, ref_sum = lax.psum((local_sums, ref_local), "rng")
    scales = lax.rsqrt(date_sums / pixel_total + 1e-06)
    ref_scale = lax.rsqrt(ref_sum / pixel_total + 1e-06)
    own_part_re = wide_re * scales[:, None, None]
    own_part_im = wide_im * scales[:, None, None]
    ref_part_re = (ref_wide_re * ref_scale)[None]
    ref_part_im = (ref_wide_im * ref_scale)[None]
    ifg_re = (own_part_re * ref_part_re + own_part_im * ref_part_im).astype(jnp.bfloat16)
    ifg_im = (own_part_im * ref_part_re - own_part_re * ref_part_im).astype(jnp.bfloat16)
    cos_table, sin_table = dft_tables(lines)
    pair = jnp.stack([ifg_re, ifg_im])
    cos_part = jnp.einsum("fl,kdlc->kdfc", cos_table, pair, preferred_element_type=jnp.float32)
    sin_part = jnp.einsum("fl,kdlc->kdfc", sin_table, pair, preferred_element_type=jnp.float32)
    spec_re = cos_part[0] + sin_part[1]
    spec_im = cos_part[1] - sin_part[0]
    weights = gain[:, None]
    held = jnp.stack(
        [(spec_re * weights).astype(jnp.bfloat16), (spec_im * weights).astype(jnp.bfloat16)]
    )
    back_cos = jnp.einsum("fl,kdfc->kdlc", cos_table, held, preferred_element_type=jnp.float32)
    back_sin = jnp.einsum("fl,kdfc->kdlc", sin_table, held, preferred_element_type=jnp.float32)
    filt_re = ((back_cos[0] - back_sin[1]) * (1.0 / lines)).astype(jnp.bfloat16)
    filt_im = ((back_sin[0] + back_cos[1]) * (1.0 / lines)).astype(jnp.bfloat16)
    phase_table = phase_tables(bperp, tdays)
    grid_size = HGRID * VGRID
    lines_dev = lines // date_axis
    my_index = lax.axis_index("date")
    piece_re = lax.all_to_all(filt_re, "date", split_axis=1, concat_axis=0, tiled=True)
    piece_im = lax.all_to_all(filt_im, "date", split_axis=1, concat_axis=0, tiled=True)
    row_count = piece_re.shape[1]
    col_count = piece_re.shape[2]
    flat_re = piece_re.reshape(piece_re.shape[0], row_count * col_count)
    flat_im = piece_im.reshape(piece_im.shape[0], row_count * col_count)
    result = coherence_map(flat_re, flat_im, phase_table)
    mapped = result.reshape(row_count, col_count, grid_size)
    mask_rows = lax.dynamic_slice_in_dim(mask, my_index * lines_dev, lines_dev, 0)
    return mapped * mask_rows.astype(jnp.float32)[:, :, None]


def solution(mesh):
    in_specs = (P("date", None, "rng"), P("date", None, "rng"), P(), P(), P(), P(), P(None, "rng"))
    out_specs = P("date", "rng", None)
    return jax.shard_map(shards, mesh=mesh, in_specs=in_specs, out_specs=out_specs, check_vma=False)
```

profile of v0, /device:TPU:1, one launch (start us, length us, event | category | flops | bytes accessed | tf_op | source)
XLA Modules:
  0.0 924.3 jit_solution(13972574443800671142)
XLA Ops:
  6.5 1.2 copy.20
  7.8 1.2 copy.21
  9.7 1.1 select_bitcast_fusion
  10.8 0.9 fusion.39
  11.7 561.3 %all-reduce.4.cloned.1.call-done = (bf16[2048,128]{0,1:T(8,128)(2,1)}, bf16[2048,128]{0,1:T(8,128)(2,1)}) async-done(((bf16[2048,128]{0,1:T(8,128)(2,1)}, bf16[2048,128]{0,1:T(8,128)(2,1)}), (bf16[2048,128]{0,1:T(8,128)(2,1)}, bf16[2048,128]{0,1:T(8,128)(2,1)})) %all-reduce.4.cloned.1.call-update) | async-done | bytes 1048592 | tf_op jit(solution)/shard_map/psum | solution.py:14
  572.9 2.1 fusion.41
  575.0 10.5 %all-reduce = (f32[]{:T(128)}, f32[1]{0:T(128)}) all-reduce(f32[]{:T(128)} %fusion.41, f32[1]{0:T(128)} %bitcast), channel_id=1, replica_groups=mesh['date'=64,'rng'=4] {'rng'}, use_global_device_ids=true, to_apply=%region_5.6 | all-reduce | flops 2 | bytes 16 | tf_op jit(solution)/shard_map/psum | solution.py:75
  587.0 1.7 fusion.59
  588.9 63.5 %fusion.18 = f32[2,1,2048,128]{2,3,0,1:T(8,128)S(1)} fusion(bf16[2,2048,128]{1,2,0:T(8,128)(2,1)S(1)} %maximum_bitcast_fusion.18), kind=kOutput, calls=%fused_computation.21 | convolution fusion | flops 2210398208 | bytes 3145728 | tf_op jit(solution)/shard_map/fl,kdlc->kdfc/dot_general | solution.py:86
  652.4 64.0 %fusion.24 = f32[2,1,2048,128]{2,3,0,1:T(8,128)S(1)} fusion(bf16[2,2048,128]{1,2,0:T(8,128)(2,1)S(1)} %maximum_bitcast_fusion.20), kind=kOutput, calls=%fused_computation.23 | convolution fusion | flops 2210398208 | bytes 3145728 | tf_op jit(solution)/shard_map/fl,kdlc->kdfc/dot_general | solution.py:87
  716.4 0.4 fusion.51
  717.0 63.2 %fusion.21 = f32[2,1,2048,128]{2,3,0,1:T(8,128)S(1)} fusion(bf16[2,2048,128]{1,2,0:T(8,128)(2,1)S(1)} %maximum_bitcast_fusion.19), kind=kOutput, calls=%fused_computation.22 | convolution fusion | flops 2210398208 | bytes 3145728 | tf_op jit(solution)/shard_map/fl,kdfc->kdlc/dot_general | solution.py:94
  780.3 63.5 %fusion.27 = f32[2,1,2048,128]{2,3,0,1:T(8,128)S(1)} fusion(bf16[2,2048,128]{1,2,0:T(8,128)(2,1)S(1)} %maximum_bitcast_fusion.21), kind=kOutput, calls=%fused_computation.24 | convolution fusion | flops 2210398208 | bytes 3145728 | tf_op jit(solution)/shard_map/fl,kdfc->kdlc/dot_general | solution.py:95
  843.8 0.4 fusion.56
  844.2 0.8 copy.25
  845.0 0.5 broadcast.173
  845.5 11.7 %reduce.6 = bf16[2048,128]{1,0:T(8,128)(2,1)S(1)} reduce(bf16[2048,1,128]{2,1,0:T(2,128)(2,1)S(1)} %bitcast.126, bf16[]{:T(256)} %broadcast.173), dimensions={1}, to_apply=%bitcast.80.reduce_sub_computation | reduce | bytes 1048578
  857.2 0.9 reshape.172
  858.2 9.5 %all-to-all-start = ((bf16[64,2,2048]{2,1,0:T(2,128)(2,1)}), bf16[64,2,2048]{2,1,0:T(2,128)(2,1)S(1)}, u32[]{:S(2)}, u32[]{:S(2)}) async-start(bf16[64,2,2048]{2,1,0:T(2,128)(2,1)} %reshape.172), calls=%async_computation | async-start | bytes 1048576 | tf_op jit(solution)/shard_map/all_to_all | solution.py:102
  867.7 0.8 copy.26
  868.4 11.5 %reduce.5 = bf16[2048,128]{1,0:T(8,128)(2,1)S(1)} reduce(bf16[2048,1,128]{2,1,0:T(2,128)(2,1)S(1)} %bitcast.127, bf16[]{:T(256)} %broadcast.173), dimensions={1}, to_apply=%bitcast.78.reduce_sub_computation | reduce | bytes 1048578
  880.0 0.9 reshape.170
  880.9 9.2 all-to-all-start.1
  890.1 0.7 dynamic-slice_convert_fusion
  891.5 0.5 reshape.173
  892.1 8.8 bitcast_reduce_fusion
  901.1 1.7 all-to-all-done.1
  902.7 0.5 reshape.171
  903.3 8.8 bitcast_reduce_fusion.1
  912.5 1.3 fusion.52
  913.8 0.8 fusion.17
  914.6 2.4 broadcast_multiply_fusion
  (20 shorter events, 1.8 us)
Async XLA Ops:
  6.5 566.4 %all-reduce.4.cloned.1.call-start = ((), (), s32[]{:S(2)}) async-start(), calls=%async_computation.2 | async-start | bytes 2097152 | tf_op jit(solution)/shard_map/psum | solution.py:14
  652.4 64.1 %copy-start = (f32[2048]{0:T(1024)S(1)}, f32[2048]{0:T(1024)}, u32[]{:S(2)}) copy-start(f32[2048]{0:T(1024)} %param.10) | copy-start | bytes 24580
  843.8 47.0 %copy-start.1 = (s32[64]{0:T(128)S(1)}, s32[64]{0:T(128)}, u32[]{:S(2)}) copy-start(s32[64]{0:T(128)} %param.12) | copy-start | bytes 772
  843.8 47.0 %copy-start.2 = (s32[64]{0:T(128)S(1)}, s32[64]{0:T(128)}, u32[]{:S(2)}) copy-start(s32[64]{0:T(128)} %param.11) | copy-start | bytes 772
  858.2 22.7 %all-to-all-start = ((bf16[64,2,2048]{2,1,0:T(2,128)(2,1)}), bf16[64,2,2048]{2,1,0:T(2,128)(2,1)S(1)}, u32[]{:S(2)}, u32[]{:S(2)}) async-start(bf16[64,2,2048]{2,1,0:T(2,128)(2,1)} %reshape.172), calls=%async_computation | async-start | bytes 1048576 | tf_op jit(solution)/shard_map/all_to_all | solution.py:102
  880.9 21.8 %all-to-all-start.1 = ((bf16[64,2,2048]{2,1,0:T(2,128)(2,1)}), bf16[64,2,2048]{2,1,0:T(2,128)(2,1)S(1)}, u32[]{:S(2)}, u32[]{:S(2)}) async-start(bf16[64,2,2048]{2,1,0:T(2,128)(2,1)} %reshape.170), calls=%async_computation.1 | async-start | bytes 1048576 | tf_op jit(solution)/shard_map/all_to_all | solution.py:103
Sparse Core Ops, SparseCore 0:
  10.9 561.9 all-reduce.3
where the time goes:
time: 932 us; the launch traced here: 924 us
  waiting for transfers between devices  563 us (60%)
  matrix products  256 us (27%)
  other arithmetic  35 us (4%)
  local copies, waits for them, and re-layouts  25.4 us (3%)
  starting transfers between devices  18.7 us (2%)
  between operations  16.2 us (2%)
  blocking collectives  10.5 us (1%)
    psum x1, waiting for transfers between devices, broadcast(): return lax.psum(jnp.where(mine, shard, jnp.zeros_like(shard)), axis)  561 us
    dot_general x1, matrix products, shards(): jnp.einsum('fl,kdlc->kdfc', sin_table, pair, preferred_element_type=jnp.f...  64 us
    dot_general x1, matrix products, shards(): jnp.einsum('fl,kdfc->kdlc', sin_table, held, preferred_element_type=jnp.f...  63.5 us
    dot_general x1, matrix products, shards(): jnp.einsum('fl,kdlc->kdfc', cos_table, pair, preferred_element_type=jnp.f...  63.5 us
    dot_general x1, matrix products, shards(): jnp.einsum('fl,kdfc->kdlc', cos_table, held, preferred_element_type=jnp.f...  63.2 us
    unnamed x2, other arithmetic  23.3 us
  transfers between devices with their start and end apart: 3, of which 2 were waited for; matrix products, arithmetic and copies ran while one was open for 3% of the time, Pallas kernels for 0%

commit v1 on v0

--- a/solution.py
+++ b/solution.py
@@ -7,6 +7,12 @@
 HGRID = 16
 VGRID = 16
 PHASE_Q = 1024
+
+
+def exchange_blocks(value, axis, split, join):
+    pieces = jnp.split(value, lax.axis_size(axis), axis=split)
+    received = lax.all_to_all(jnp.stack(pieces), axis, 0, 0)
+    return jnp.concatenate(received, axis=join)
 
 
 def broadcast(shard, axis, root):
@@ -100,7 +106,7 @@
     lines_dev = lines // date_axis
     my_index = lax.axis_index("date")
     piece_re = lax.all_to_all(filt_re, "date", split_axis=1, concat_axis=0, tiled=True)
-    piece_im = lax.all_to_all(filt_im, "date", split_axis=1, concat_axis=0, tiled=True)
+    piece_im = exchange_blocks(filt_im, "date", 1, 0)
     row_count = piece_re.shape[1]
     col_count = piece_re.shape[2]
     flat_re = piece_re.reshape(piece_re.shape[0], row_count * col_count)

time: 932 us -> 955 us (1.025)
  local copies, waits for them, and re-layouts: 25.4 us -> 59.3 us
  other arithmetic: 35 us -> 23.6 us
    unnamed x13 -> x75, local copies, waits for them, and re-layouts: 5.92 us -> 42.6 us
    unnamed x2 -> x1, other arithmetic: 23.3 us -> 11.7 us
  transfers between devices with their start and end apart: 3 -> 3, of which waited for: 2 -> 2; matrix products, arithmetic and copies ran while one was open for 3% -> 5% of each run, Pallas kernels for 0% -> 0%
where the time goes in v1:
time: 955 us; the launch traced here: 947 us
  waiting for transfers between devices  563 us (59%)
  matrix products  256 us (27%)
  local copies, waits for them, and re-layouts  59.3 us (6%)
  other arithmetic  23.6 us (2%)
  starting transfers between devices  18.7 us (2%)
  between operations  16.2 us (2%)
  blocking collectives  10.5 us (1%)
    psum x1, waiting for transfers between devices, broadcast(): return lax.psum(jnp.where(mine, shard, jnp.zeros_like(shard)), axis)  561 us
    dot_general x1, matrix products, shards(): jnp.einsum('fl,kdlc->kdfc', sin_table, pair, preferred_element_type=jnp.f...  64.1 us
    dot_general x1, matrix products, shards(): jnp.einsum('fl,kdfc->kdlc', sin_table, held, preferred_element_type=jnp.f...  63.5 us
    dot_general x1, matrix products, shards(): jnp.einsum('fl,kdlc->kdfc', cos_table, pair, preferred_element_type=jnp.f...  63.5 us
    dot_general x1, matrix products, shards(): jnp.einsum('fl,kdfc->kdlc', cos_table, held, preferred_element_type=jnp.f...  63.2 us
    unnamed x75, local copies, waits for them, and re-layouts  42.6 us
  transfers between devices with their start and end apart: 3, of which 2 were waited for; matrix products, arithmetic and copies ran while one was open for 5% of the time, Pallas kernels for 0%

profile of v1, /device:TPU:1, one launch (start us, length us, event | category | flops | bytes accessed | tf_op | source)
XLA Modules:
  0.0 946.7 jit_solution(3790334989144324326)
XLA Ops:
  6.5 1.2 copy.20
  7.8 1.2 copy.21
  9.7 1.0 select_bitcast_fusion
  10.8 0.9 fusion.39
  11.7 561.2 %all-reduce.4.cloned.1.call-done = (bf16[2048,128]{0,1:T(8,128)(2,1)}, bf16[2048,128]{0,1:T(8,128)(2,1)}) async-done(((bf16[2048,128]{0,1:T(8,128)(2,1)}, bf16[2048,128]{0,1:T(8,128)(2,1)}), (bf16[2048,128]{0,1:T(8,128)(2,1)}, bf16[2048,128]{0,1:T(8,128)(2,1)})) %all-reduce.4.cloned.1.call-update) | async-done | bytes 1048592 | tf_op jit(solution)/shard_map/psum | solution.py:20
  572.9 2.1 fusion.41
  575.0 10.5 %all-reduce = (f32[]{:T(128)}, f32[1]{0:T(128)}) all-reduce(f32[]{:T(128)} %fusion.41, f32[1]{0:T(128)} %bitcast), channel_id=1, replica_groups=mesh['date'=64,'rng'=4] {'rng'}, use_global_device_ids=true, to_apply=%region_5.6 | all-reduce | flops 2 | bytes 16 | tf_op jit(solution)/shard_map/psum | solution.py:81
  586.9 1.7 fusion.59
  588.8 63.5 %fusion.18 = f32[2,1,2048,128]{2,3,0,1:T(8,128)S(1)} fusion(bf16[2,2048,128]{1,2,0:T(8,128)(2,1)S(1)} %maximum_bitcast_fusion.18), kind=kOutput, calls=%fused_computation.21 | convolution fusion | flops 2210398208 | bytes 3145728 | tf_op jit(solution)/shard_map/fl,kdlc->kdfc/dot_general | solution.py:92
  652.3 64.1 %fusion.24 = f32[2,1,2048,128]{2,3,0,1:T(8,128)S(1)} fusion(bf16[2,2048,128]{1,2,0:T(8,128)(2,1)S(1)} %maximum_bitcast_fusion.20), kind=kOutput, calls=%fused_computation.23 | convolution fusion | flops 2210398208 | bytes 3145728 | tf_op jit(solution)/shard_map/fl,kdlc->kdfc/dot_general | solution.py:93
  717.0 63.2 %fusion.21 = f32[2,1,2048,128]{2,3,0,1:T(8,128)S(1)} fusion(bf16[2,2048,128]{1,2,0:T(8,128)(2,1)S(1)} %maximum_bitcast_fusion.19), kind=kOutput, calls=%fused_computation.22 | convolution fusion | flops 2210398208 | bytes 3145728 | tf_op jit(solution)/shard_map/fl,kdfc->kdlc/dot_general | solution.py:100
  780.2 63.5 %fusion.27 = f32[2,1,2048,128]{2,3,0,1:T(8,128)S(1)} fusion(bf16[2,2048,128]{1,2,0:T(8,128)(2,1)S(1)} %maximum_bitcast_fusion.21), kind=kOutput, calls=%fused_computation.24 | convolution fusion | flops 2210398208 | bytes 3145728 | tf_op jit(solution)/shard_map/fl,kdfc->kdlc/dot_general | solution.py:101
  845.0 0.6 constant_dynamic-update-slice_fusion.63
  850.5 0.8 copy.25
  851.8 11.7 %reduce.3 = bf16[2048,128]{1,0:T(8,128)(2,1)S(1)} reduce(bf16[2048,1,128]{2,1,0:T(2,128)(2,1)S(1)} %bitcast.260, bf16[]{:T(256)} %broadcast.172), dimensions={1}, to_apply=%bitcast.212.reduce_sub_computation | reduce | bytes 1048578
  863.6 0.9 reshape.165
  864.5 9.5 %all-to-all-start = ((bf16[64,2,2048]{2,1,0:T(2,128)(2,1)}), bf16[64,2,2048]{2,1,0:T(2,128)(2,1)S(1)}, u32[]{:S(2)}, u32[]{:S(2)}) async-start(bf16[64,2,2048]{2,1,0:T(2,128)(2,1)} %reshape.165), calls=%async_computation | async-start | bytes 1048576 | tf_op jit(solution)/shard_map/all_to_all | solution.py:108
  874.0 0.6 constant_dynamic-update-slice_fusion.62
  874.6 0.6 constant_dynamic-update-slice_fusion.61
  876.4 0.6 constant_dynamic-update-slice_fusion.58
  878.2 0.6 constant_dynamic-update-slice_fusion.55
  878.8 0.6 constant_dynamic-update-slice_fusion.54
  880.6 0.6 constant_dynamic-update-slice_fusion.51
  882.4 0.6 constant_dynamic-update-slice_fusion.48
  907.1 0.6 constant_dynamic-update-slice_fusion.8
  912.6 9.2 all-to-all-start.1
  921.8 0.7 dynamic-slice_convert_fusion
  923.7 8.8 bitcast_reduce_fusion
  932.7 1.7 all-to-all-done.1
  935.0 1.3 fusion.52
  936.2 0.8 fusion.17
  937.0 2.4 broadcast_multiply_fusion
  (147 shorter events, 43.1 us)
Async XLA Ops:
  6.5 566.4 %all-reduce.4.cloned.1.call-start = ((), (), s32[]{:S(2)}) async-start(), calls=%async_computation.2 | async-start | bytes 2097152 | tf_op jit(solution)/shard_map/psum | solution.py:20
  652.3 64.1 %copy-start = (f32[2048]{0:T(1024)S(1)}, f32[2048]{0:T(1024)}, u32[]{:S(2)}) copy-start(f32[2048]{0:T(1024)} %param.10) | copy-start | bytes 24580
  844.1 78.4 %copy-start.1 = (s32[64]{0:T(128)S(1)}, s32[64]{0:T(128)}, u32[]{:S(2)}) copy-start(s32[64]{0:T(128)} %param.12) | copy-start | bytes 772
  844.1 78.4 %copy-start.2 = (s32[64]{0:T(128)S(1)}, s32[64]{0:T(128)}, u32[]{:S(2)}) copy-start(s32[64]{0:T(128)} %param.11) | copy-start | bytes 772
  864.5 48.1 %all-to-all-start = ((bf16[64,2,2048]{2,1,0:T(2,128)(2,1)}), bf16[64,2,2048]{2,1,0:T(2,128)(2,1)S(1)}, u32[]{:S(2)}, u32[]{:S(2)}) async-start(bf16[64,2,2048]{2,1,0:T(2,128)(2,1)} %reshape.165), calls=%async_computation | async-start | bytes 1048576 | tf_op jit(solution)/shard_map/all_to_all | solution.py:108
  912.6 21.8 %all-to-all-start.1 = ((bf16[64,1,32,128]{3,2,1,0:T(8,128)(2,1)}), bf16[64,1,32,128]{3,2,1,0:T(8,128)(2,1)S(1)}, u32[]{:S(2)}, u32[]{:S(2)}) async-start(bf16[64,1,32,128]{3,2,1,0:T(8,128)(2,1)} %constant_dynamic-update-slice_fusion), calls=%async_computation.1 | async-start | bytes 1048576 | tf_op jit(solution)/shard_map/all_to_all | solution.py:14
Sparse Core Ops, SparseCore 0:
  10.9 561.9 all-reduce.3
